TPU v7x, 512 devices: a whole 4x8x8 slice. The times are simulated.
512 devices in a mesh: grid: 64 (over x, z, core), orb: 8 (over y).
Axes of the slice: x: 4, y: 8, z: 8, core: 2. Of those that a mesh axis runs over, the one named last changes fastest.
Arguments:
- orbitals: float32 [256, 16, 16, 1024], P('grid', None, None, 'orb'), may hold values from -15 to 15
- potential: float32 [256, 16, 16], P('grid'), may hold values from -2 to 0
Outputs:
- filtered: float32 [256, 16, 16, 1024], P('grid', None, None, 'orb')
- hamiltonian_block: float32 [1024, 1024], P('orb', 'grid')
- margin_block: float32 [1024, 1024], P('orb', 'grid')
All inputs are finite; a program needn't handle non-finite values.
Results may differ from a plain program's by a relative error of at most 0.0039.
Values may be sent and summed in bfloat16 or wider, within the bound.
No kernel may reach another device: no remote copies, remote signals or barrier semaphores. Data moves between devices by JAX's collectives and lax.ppermute only.
A program may use at most 64 MiB of HBM per device.

v0:
```python
import jax
import jax.numpy as jnp
from jax import lax
from jax.sharding import PartitionSpec as P

DEGREE = 4
STENCIL = (-205.0 / 72.0, 8.0 / 5.0, -1.0 / 5.0, 8.0 / 315.0, -1.0 / 560.0)
LOWER_EDGE = -2.0
CUT_EDGE = 1.5
UPPER_EDGE = 10.0
EPSILON = 1e-06


def halo_layers(shard, width):
    size = lax.axis_size("grid")
    length = shard.shape[0]
    up = [(i, i + 1) for i in range(size - 1)]
    down = [(j, i) for i, j in up]
    last = lax.slice_in_dim(shard, length - width, length, axis=0).astype(jnp.bfloat16)
    initial = lax.slice_in_dim(shard, 0, width, axis=0).astype(jnp.bfloat16)
    before = lax.ppermute(last, "grid", up).astype(shard.dtype)
    after = lax.ppermute(initial, "grid", down).astype(shard.dtype)
    return jnp.concatenate([before, shard, after], axis=0)


def plane_matrix(rows_y, cols_x):
    flat_count = rows_y * cols_x
    index_all = jnp.arange(flat_count, dtype=jnp.int32)
    row_y = (index_all // cols_x)[:, None]
    row_x = (index_all % cols_x)[:, None]
    col_y = (index_all // cols_x)[None, :]
    col_x = (index_all % cols_x)[None, :]
    delta_y = jnp.mod(row_y - col_y, rows_y)
    delta_x = jnp.mod(row_x - col_x, cols_x)
    same_y = delta_y == 0
    same_x = delta_x == 0
    matrix = jnp.zeros((flat_count, flat_count), jnp.float32)
    for offset in range(1, 5):
        for signed in (offset, -offset):
            hit_y = jnp.logical_and(same_x, delta_y == signed % rows_y)
            hit_x = jnp.logical_and(same_y, delta_x == signed % cols_x)
            matrix = matrix + STENCIL[offset] * (
                hit_y.astype(jnp.float32) + hit_x.astype(jnp.float32)
            )
    return matrix


def apply_hamiltonian(current, potential, plane):
    layers, rows_y, cols_x, width = current.shape
    padded = halo_layers(current, 4)
    laplacian = 3.0 * STENCIL[0] * current
    for offset in range(1, 5):
        laplacian = laplacian + STENCIL[offset] * (
            padded[4 + offset : 4 + offset + layers] + padded[4 - offset : 4 - offset + layers]
        )
    flat = current.reshape(layers, rows_y * cols_x, width)
    in_plane = jnp.einsum(
        "pq,zqo->zpo",
        plane,
        flat,
        precision=lax.Precision.HIGHEST,
        preferred_element_type=jnp.float32,
    )
    laplacian = laplacian + in_plane.reshape(current.shape)
    return -0.5 * laplacian + potential[:, :, :, None] * current


def chebyshev(initial, potential, plane):
    half_width = (UPPER_EDGE - CUT_EDGE) / 2.0
    centre = (UPPER_EDGE + CUT_EDGE) / 2.0
    sigma_now = half_width / (LOWER_EDGE - centre)
    gamma_ratio = 2.0 / sigma_now
    previous = initial
    current = (
        sigma_now / half_width * (apply_hamiltonian(previous, potential, plane) - centre * previous)
    )
    for degree_step in range(DEGREE - 1):
        sigma_next = 1.0 / (gamma_ratio - sigma_now)
        following = (
            2.0
            * sigma_next
            / half_width
            * (apply_hamiltonian(current, potential, plane) - centre * current)
            - sigma_now * sigma_next * previous
        )
        previous, current, sigma_now = (current, following, sigma_next)
    return current


def contract_points(left_side, right_side):
    return lax.dot_general(
        left_side, right_side, (((0,), (0,)), ((), ())), preferred_element_type=jnp.float32
    )


def reduce_scatter_grid(slots):
    size = slots.shape[0]
    bits = size.bit_length() - 1
    me = lax.axis_index("grid")
    rest = slots.shape[1:]
    buf = slots.reshape((2,) * bits + rest)
    for bit in range(bits):
        axis = bits - 1 - bit
        mine = me >> bit & 1
        low = lax.index_in_dim(buf, 0, axis=axis, keepdims=False)
        high = lax.index_in_dim(buf, 1, axis=axis, keepdims=False)
        keep = jnp.where(mine == 1, high, low)
        send = jnp.where(mine == 1, low, high)
        pairs = [(i, i ^ 1 << bit) for i in range(size)]
        buf = keep + lax.ppermute(send, "grid", pairs)
    return buf


def on_device(orbitals, potential):
    own_width = orbitals.shape[3]
    point_count = orbitals.shape[0] * orbitals.shape[1] * orbitals.shape[2]
    grid_size = lax.axis_size("grid")
    point_total = float(point_count * grid_size)
    plane = plane_matrix(orbitals.shape[1], orbitals.shape[2])
    result_block = chebyshev(orbitals, potential, plane)
    own_squares = jnp.sum(result_block * result_block, axis=(0, 1, 2))
    rounded_orbitals = result_block.astype(jnp.bfloat16).reshape(point_count, own_width)
    rounded_image = (
        apply_hamiltonian(result_block, potential, plane)
        .astype(jnp.bfloat16)
        .reshape(point_count, own_width)
    )
    orbitals_all = lax.all_gather(rounded_orbitals, "orb", axis=1, tiled=True)
    total_width = orbitals_all.shape[1]
    rows = total_width // grid_size
    hamiltonian_part = contract_points(orbitals_all, rounded_image)
    margin_part = contract_points(orbitals_all, rounded_orbitals)
    wide = orbitals_all.astype(jnp.float32)
    column_squares = jnp.sum(wide * wide, axis=0)
    body = jnp.concatenate(
        [
            hamiltonian_part.reshape(grid_size, rows, own_width),
            margin_part.reshape(grid_size, rows, own_width),
        ],
        axis=2,
    )
    tail = jnp.concatenate(
        [
            column_squares.reshape(grid_size, rows),
            jnp.broadcast_to(own_squares[None, :], (grid_size, own_width)),
            jnp.zeros((grid_size, own_width - rows), jnp.float32),
        ],
        axis=1,
    )
    slots = jnp.concatenate([body, tail[:, None, :]], axis=1)
    combined = reduce_scatter_grid(slots)
    scale_own = 1.0 / jnp.sqrt(combined[rows, rows : rows + own_width] / point_total + EPSILON)
    column_scale = 1.0 / jnp.sqrt(combined[rows, :rows] / point_total + EPSILON)
    filtered = result_block * scale_own
    pair_scale = scale_own[:, None] * column_scale[None, :] / point_total
    hamiltonian_block = combined[:rows, :own_width].T * pair_scale
    margin_block = combined[:rows, own_width:].T * pair_scale
    return (filtered, hamiltonian_block, margin_block)


def solution(mesh):
    placed = (P("grid", None, None, "orb"), P("grid", None, None))
    return jax.shard_map(
        on_device,
        mesh=mesh,
        in_specs=placed,
        out_specs=(P("grid", None, None, "orb"), P("orb", "grid"), P("orb", "grid")),
        check_vma=False,
    )
```

profile of v0, /device:TPU:2, one launch (start us, length us, event | category | flops | bytes accessed | tf_op | source)
XLA Modules:
  0.0 181.1 jit_solution(14058231074587495252)
XLA Ops:
  8.3 10.4 %collective-permute-start = (bf16[4,16,16,128]{3,2,1,0:T(8,128)(2,1)S(1)}, bf16[4,16,16,128]{3,2,1,0:T(8,128)(2,1)S(1)}, u32[]{:S(2)}, u32[]{:S(2)}) collective-permute-start(bf16[4,16,16,128]{3,2,1,0:T(8,128)(2,1)S(1)} %convert_element_type.233), channel_id=1, source_target_pairs={{8,0},{16,8},{24,16},{32,24},{40,32},{48,40},{56,48},{64,56},{72,6... | collective-permute-start | bytes 786440 | tf_op jit(solution)/shard_map/ppermute | solution.py:22
  21.4 2.7 %fusion.102 = f32[256,4,128]{2,0,1:T(8,128)S(1)} fusion(f32[4,256,128]{2,1,0:T(8,128)} %bitcast.96, s32[256]{0:T(256)S(1)} %get-tuple-element.22, s32[256]{0:T(256)S(1)} %get-tuple-element.23), kind=kOutput, calls=%fused_computation.176 | convolution fusion | flops 408944640 | bytes 1050624 | tf_op jit(solution)/shard_map/pq,zqo->zpo/dot_general | solution.py:57
  24.2 4.3 %collective-permute-done.1 = bf16[4,16,16,128]{3,2,1,0:T(8,128)(2,1)S(1)} collective-permute-done((bf16[4,16,16,128]{3,2,1,0:T(8,128)(2,1)S(1)}, bf16[4,16,16,128]{3,2,1,0:T(8,128)(2,1)S(1)}, u32[]{:S(2)}, u32[]{:S(2)}) %collective-permute-start.1) | collective-permute-done | bytes 262176 | tf_op jit(solution)/shard_map/ppermute | solution.py:21
  30.8 2.4 %collective-permute-start.3 = (bf16[4,16,16,128]{3,2,1,0:T(8,128)(2,1)S(1)}, bf16[4,16,16,128]{3,2,1,0:T(8,128)(2,1)S(1)}, u32[]{:S(2)}, u32[]{:S(2)}) collective-permute-start(bf16[4,16,16,128]{3,2,1,0:T(8,128)(2,1)S(1)} %get-tuple-element.9), channel_id=1, source_target_pairs={{0,8},{8,16},{16,24},{24,32},{32,40},{40,48},{48,56},{56,64},{64,7... | collective-permute-start | bytes 786440 | tf_op jit(solution)/shard_map/ppermute | solution.py:21
  35.5 5.1 %collective-permute-done.3 = bf16[4,16,16,128]{3,2,1,0:T(8,128)(2,1)S(1)} collective-permute-done((bf16[4,16,16,128]{3,2,1,0:T(8,128)(2,1)S(1)}, bf16[4,16,16,128]{3,2,1,0:T(8,128)(2,1)S(1)}, u32[]{:S(2)}, u32[]{:S(2)}) %collective-permute-start.3) | collective-permute-done | bytes 262176 | tf_op jit(solution)/shard_map/ppermute | solution.py:21
  43.1 2.4 %collective-permute-start.5 = (bf16[4,16,16,128]{3,2,1,0:T(8,128)(2,1)S(1)}, bf16[4,16,16,128]{3,2,1,0:T(8,128)(2,1)S(1)}, u32[]{:S(2)}, u32[]{:S(2)}) collective-permute-start(bf16[4,16,16,128]{3,2,1,0:T(8,128)(2,1)S(1)} %get-tuple-element.7), channel_id=1, source_target_pairs={{0,8},{8,16},{16,24},{24,32},{32,40},{40,48},{48,56},{56,64},{64,7... | collective-permute-start | bytes 786440 | tf_op jit(solution)/shard_map/ppermute | solution.py:21
  45.5 1.9 %convolution_bitcast_fusion.2 = f32[4,256,128]{1,2,0:T(8,128)S(1)} fusion(f32[4,256,128]{2,1,0:T(8,128)S(1)} %bitcast.97, s32[256]{0:T(256)S(1)} %get-tuple-element.22, s32[256]{0:T(256)S(1)} %get-tuple-element.23), kind=kOutput, calls=%fused_computation.43 | convolution fusion | flops 408944640 | bytes 1050624 | tf_op jit(solution)/shard_map/pq,zqo->zpo/dot_general | solution.py:57
  47.7 5.2 %collective-permute-done.5 = bf16[4,16,16,128]{3,2,1,0:T(8,128)(2,1)S(1)} collective-permute-done((bf16[4,16,16,128]{3,2,1,0:T(8,128)(2,1)S(1)}, bf16[4,16,16,128]{3,2,1,0:T(8,128)(2,1)S(1)}, u32[]{:S(2)}, u32[]{:S(2)}) %collective-permute-start.5) | collective-permute-done | bytes 262176 | tf_op jit(solution)/shard_map/ppermute | solution.py:21
  55.2 2.4 %collective-permute-start.7 = (bf16[4,16,16,128]{3,2,1,0:T(8,128)(2,1)S(1)}, bf16[4,16,16,128]{3,2,1,0:T(8,128)(2,1)S(1)}, u32[]{:S(2)}, u32[]{:S(2)}) collective-permute-start(bf16[4,16,16,128]{3,2,1,0:T(8,128)(2,1)S(1)} %get-tuple-element.5), channel_id=1, source_target_pairs={{0,8},{8,16},{16,24},{24,32},{32,40},{40,48},{48,56},{56,64},{64,7... | collective-permute-start | bytes 786440 | tf_op jit(solution)/shard_map/ppermute | solution.py:21
  59.8 5.2 %collective-permute-done.7 = bf16[4,16,16,128]{3,2,1,0:T(8,128)(2,1)S(1)} collective-permute-done((bf16[4,16,16,128]{3,2,1,0:T(8,128)(2,1)S(1)}, bf16[4,16,16,128]{3,2,1,0:T(8,128)(2,1)S(1)}, u32[]{:S(2)}, u32[]{:S(2)}) %collective-permute-start.7) | collective-permute-done | bytes 262176 | tf_op jit(solution)/shard_map/ppermute | solution.py:21
  68.3 5.9 %collective-permute-start.8 = (bf16[4,16,16,128]{3,2,1,0:T(8,128)(2,1)}, bf16[4,16,16,128]{3,2,1,0:T(8,128)(2,1)S(1)}, u32[]{:S(2)}, u32[]{:S(2)}) collective-permute-start(bf16[4,16,16,128]{3,2,1,0:T(8,128)(2,1)} %convert_element_type.261), channel_id=1, source_target_pairs={{8,0},{16,8},{24,16},{32,24},{40,32},{48,40},{56,48},{64,56},{72,6... | collective-permute-start | bytes 786440 | tf_op jit(solution)/shard_map/ppermute | solution.py:22
  78.6 34.1 %all-gather.2.cloned.1.call-done = bf16[1024,1024]{1,0:T(8,128)(2,1)} async-done(((bf16[1024,128]{1,0:T(8,128)(2,1)}), bf16[1024,1024]{1,0:T(8,128)(2,1)}) %all-gather.2.cloned.1.call-update) | async-done | bytes 2097168 | tf_op jit(solution)/shard_map/all_gather | solution.py:128
  112.8 2.1 %multiply_reduce_fusion = f32[1024]{0:T(1024)S(1)} fusion(bf16[1024,1024]{1,0:T(8,128)(2,1)} %all-gather.2.cloned.1.call-done), kind=kLoop, calls=%fused_computation | loop fusion | flops 3144704 | bytes 2101248 | tf_op jit(solution)/shard_map/reduce_sum | solution.py:134
  115.0 2.9 %copy.191 = bf16[1024,1024]{1,0:T(8,128)(2,1)S(1)} copy(bf16[1024,1024]{0,1:T(8,128)(2,1)} %bitcast.94) | data formatting | bytes 4194304 | tf_op jit(solution)/shard_map/dot_general | solution.py:91
  124.3 2.1 %collective-permute-done.10 = f32[2,2,2,2,2,17,256]{6,4,5,3,2,1,0:T(2,128)S(1)} collective-permute-done((f32[2,2,2,2,2,17,256]{6,4,5,3,2,1,0:T(2,128)}, f32[2,2,2,2,2,17,256]{6,4,5,3,2,1,0:T(2,128)S(1)}, u32[]{:S(2)}, u32[]{:S(2)}) %collective-permute-start.10) | collective-permute-done | bytes 557088 | tf_op jit(solution)/shard_map/ppermute | solution.py:110
  127.0 3.6 %collective-permute-start.11 = (f32[2,2,2,2,17,256]{5,3,4,2,1,0:T(2,128)S(1)}, f32[2,2,2,2,17,256]{5,3,4,2,1,0:T(2,128)S(1)}, u32[]{:S(2)}, u32[]{:S(2)}) collective-permute-start(f32[2,2,2,2,17,256]{5,3,4,2,1,0:T(2,128)S(1)} %select_bitcast_fusion.1), channel_id=1, source_target_pairs={{0,16},{8,24},{16,0},{24,8},{32,48},{40,56},{48,32},{56,40},{64,80... | collective-permute-start | bytes 835592 | tf_op jit(solution)/shard_map/ppermute | solution.py:110
  130.6 7.0 %collective-permute-done.11 = f32[2,2,2,2,17,256]{5,3,4,2,1,0:T(2,128)S(1)} collective-permute-done((f32[2,2,2,2,17,256]{5,3,4,2,1,0:T(2,128)S(1)}, f32[2,2,2,2,17,256]{5,3,4,2,1,0:T(2,128)S(1)}, u32[]{:S(2)}, u32[]{:S(2)}) %collective-permute-start.11) | collective-permute-done | bytes 278560 | tf_op jit(solution)/shard_map/ppermute | solution.py:110
  138.1 4.6 %collective-permute-start.12 = (f32[2,2,2,17,256]{4,2,3,1,0:T(2,128)S(1)}, f32[2,2,2,17,256]{4,2,3,1,0:T(2,128)S(1)}, u32[]{:S(2)}, u32[]{:S(2)}) collective-permute-start(f32[2,2,2,17,256]{4,2,3,1,0:T(2,128)S(1)} %bitcast.109), channel_id=1, source_target_pairs={{0,32},{8,40},{16,48},{24,56},{32,0},{40,8},{48,16},{56,24},{64,96... | collective-permute-start | bytes 417800 | tf_op jit(solution)/shard_map/ppermute | solution.py:110
  142.8 6.1 %collective-permute-done.12 = f32[2,2,2,17,256]{4,2,3,1,0:T(2,128)S(1)} collective-permute-done((f32[2,2,2,17,256]{4,2,3,1,0:T(2,128)S(1)}, f32[2,2,2,17,256]{4,2,3,1,0:T(2,128)S(1)}, u32[]{:S(2)}, u32[]{:S(2)}) %collective-permute-start.12) | collective-permute-done | bytes 139296 | tf_op jit(solution)/shard_map/ppermute | solution.py:110
  149.1 7.9 %collective-permute-start.13 = (f32[2,2,17,256]{3,1,2,0:T(2,128)S(1)}, f32[2,2,17,256]{3,1,2,0:T(2,128)S(1)}, u32[]{:S(2)}, u32[]{:S(2)}) collective-permute-start(f32[2,2,17,256]{3,1,2,0:T(2,128)S(1)} %bitcast.110), channel_id=1, source_target_pairs={{0,64},{8,72},{16,80},{24,88},{32,96},{40,104},{48,112},{56,120},{... | collective-permute-start | bytes 208904 | tf_op jit(solution)/shard_map/ppermute | solution.py:110
  157.0 2.3 %collective-permute-done.13 = f32[2,2,17,256]{3,1,2,0:T(2,128)S(1)} collective-permute-done((f32[2,2,17,256]{3,1,2,0:T(2,128)S(1)}, f32[2,2,17,256]{3,1,2,0:T(2,128)S(1)}, u32[]{:S(2)}, u32[]{:S(2)}) %collective-permute-start.13) | collective-permute-done | bytes 69664 | tf_op jit(solution)/shard_map/ppermute | solution.py:110
  159.5 4.0 %collective-permute-start.14 = (f32[2,17,256]{2,0,1:T(2,128)S(1)}, f32[2,17,256]{2,0,1:T(2,128)S(1)}, u32[]{:S(2)}, u32[]{:S(2)}) collective-permute-start(f32[2,17,256]{2,0,1:T(2,128)S(1)} %bitcast.111), channel_id=1, source_target_pairs={{0,128},{8,136},{16,144},{24,152},{32,160},{40,168},{48,176},{56,1... | collective-permute-start | bytes 104456 | tf_op jit(solution)/shard_map/ppermute | solution.py:110
  165.5 3.9 %collective-permute-start.15 = (f32[17,256]{1,0:T(8,128)S(1)}, f32[17,256]{1,0:T(8,128)S(1)}, u32[]{:S(2)}, u32[]{:S(2)}) collective-permute-start(f32[17,256]{1,0:T(8,128)S(1)} %bitcast.112), channel_id=1, source_target_pairs={{0,256},{8,264},{16,272},{24,280},{32,288},{40,296},{48,304},{56,3... | collective-permute-start | bytes 52232 | tf_op jit(solution)/shard_map/ppermute | solution.py:110
  169.4 3.3 %collective-permute-done.15 = f32[17,256]{1,0:T(8,128)S(1)} collective-permute-done((f32[17,256]{1,0:T(8,128)S(1)}, f32[17,256]{1,0:T(8,128)S(1)}, u32[]{:S(2)}, u32[]{:S(2)}) %collective-permute-start.15) | collective-permute-done | bytes 17440 | tf_op jit(solution)/shard_map/ppermute | solution.py:110
  (79 shorter events, 34.6 us)
Async XLA Ops:
  7.2 105.6 %all-gather.2.cloned.1.call-start = ((), (), s32[]{:S(2)}) async-start(), calls=%async_computation | async-start | bytes 2359296 | tf_op jit(solution)/shard_map/all_gather | solution.py:128
  8.3 15.8 %collective-permute-start = (bf16[4,16,16,128]{3,2,1,0:T(8,128)(2,1)S(1)}, bf16[4,16,16,128]{3,2,1,0:T(8,128)(2,1)S(1)}, u32[]{:S(2)}, u32[]{:S(2)}) collective-permute-start(bf16[4,16,16,128]{3,2,1,0:T(8,128)(2,1)S(1)} %convert_element_type.233), channel_id=1, source_target_pairs={{8,0},{16,8},{24,16},{32,24},{40,32},{48,40},{56,48},{64,56},{72,6... | collective-permute-start | bytes 786440 | tf_op jit(solution)/shard_map/ppermute | solution.py:22
  18.7 9.8 %collective-permute-start.1 = (bf16[4,16,16,128]{3,2,1,0:T(8,128)(2,1)S(1)}, bf16[4,16,16,128]{3,2,1,0:T(8,128)(2,1)S(1)}, u32[]{:S(2)}, u32[]{:S(2)}) collective-permute-start(bf16[4,16,16,128]{3,2,1,0:T(8,128)(2,1)S(1)} %convert_element_type.233), channel_id=1, source_target_pairs={{0,8},{8,16},{16,24},{24,32},{32,40},{40,48},{48,56},{56,64},{64,7... | collective-permute-start | bytes 786440 | tf_op jit(solution)/shard_map/ppermute | solution.py:21
  21.4 7.1 %copy-start = (f32[4,16,16,128]{3,2,1,0:T(8,128)S(1)}, f32[4,16,16,128]{3,2,1,0:T(8,128)}, u32[]{:S(2)}) copy-start(f32[4,16,16,128]{3,2,1,0:T(8,128)} %param.2) | copy-start | bytes 1572868
  21.4 7.2 %copy-start.2 = (f32[4,16,16]{2,1,0:T(8,128)S(1)}, f32[4,16,16]{2,1,0:T(8,128)}, u32[]{:S(2)}) copy-start(f32[4,16,16]{2,1,0:T(8,128)} %param.3) | copy-start | bytes 12292
  28.9 6.5 %collective-permute-start.2 = (bf16[4,16,16,128]{3,2,1,0:T(8,128)(2,1)S(1)}, bf16[4,16,16,128]{3,2,1,0:T(8,128)(2,1)S(1)}, u32[]{:S(2)}, u32[]{:S(2)}) collective-permute-start(bf16[4,16,16,128]{3,2,1,0:T(8,128)(2,1)S(1)} %get-tuple-element.9), channel_id=1, source_target_pairs={{8,0},{16,8},{24,16},{32,24},{40,32},{48,40},{56,48},{64,56},{72,6... | collective-permute-start | bytes 786440 | tf_op jit(solution)/shard_map/ppermute | solution.py:22
  30.8 9.8 %collective-permute-start.3 = (bf16[4,16,16,128]{3,2,1,0:T(8,128)(2,1)S(1)}, bf16[4,16,16,128]{3,2,1,0:T(8,128)(2,1)S(1)}, u32[]{:S(2)}, u32[]{:S(2)}) collective-permute-start(bf16[4,16,16,128]{3,2,1,0:T(8,128)(2,1)S(1)} %get-tuple-element.9), channel_id=1, source_target_pairs={{0,8},{8,16},{16,24},{24,32},{32,40},{40,48},{48,56},{56,64},{64,7... | collective-permute-start | bytes 786440 | tf_op jit(solution)/shard_map/ppermute | solution.py:21
  41.1 6.5 %collective-permute-start.4 = (bf16[4,16,16,128]{3,2,1,0:T(8,128)(2,1)S(1)}, bf16[4,16,16,128]{3,2,1,0:T(8,128)(2,1)S(1)}, u32[]{:S(2)}, u32[]{:S(2)}) collective-permute-start(bf16[4,16,16,128]{3,2,1,0:T(8,128)(2,1)S(1)} %get-tuple-element.7), channel_id=1, source_target_pairs={{8,0},{16,8},{24,16},{32,24},{40,32},{48,40},{56,48},{64,56},{72,6... | collective-permute-start | bytes 786440 | tf_op jit(solution)/shard_map/ppermute | solution.py:22
  43.1 9.8 %collective-permute-start.5 = (bf16[4,16,16,128]{3,2,1,0:T(8,128)(2,1)S(1)}, bf16[4,16,16,128]{3,2,1,0:T(8,128)(2,1)S(1)}, u32[]{:S(2)}, u32[]{:S(2)}) collective-permute-start(bf16[4,16,16,128]{3,2,1,0:T(8,128)(2,1)S(1)} %get-tuple-element.7), channel_id=1, source_target_pairs={{0,8},{8,16},{16,24},{24,32},{32,40},{40,48},{48,56},{56,64},{64,7... | collective-permute-start | bytes 786440 | tf_op jit(solution)/shard_map/ppermute | solution.py:21
  53.3 6.5 %collective-permute-start.6 = (bf16[4,16,16,128]{3,2,1,0:T(8,128)(2,1)S(1)}, bf16[4,16,16,128]{3,2,1,0:T(8,128)(2,1)S(1)}, u32[]{:S(2)}, u32[]{:S(2)}) collective-permute-start(bf16[4,16,16,128]{3,2,1,0:T(8,128)(2,1)S(1)} %get-tuple-element.5), channel_id=1, source_target_pairs={{8,0},{16,8},{24,16},{32,24},{40,32},{48,40},{56,48},{64,56},{72,6... | collective-permute-start | bytes 786440 | tf_op jit(solution)/shard_map/ppermute | solution.py:22
  55.2 9.8 %collective-permute-start.7 = (bf16[4,16,16,128]{3,2,1,0:T(8,128)(2,1)S(1)}, bf16[4,16,16,128]{3,2,1,0:T(8,128)(2,1)S(1)}, u32[]{:S(2)}, u32[]{:S(2)}) collective-permute-start(bf16[4,16,16,128]{3,2,1,0:T(8,128)(2,1)S(1)} %get-tuple-element.5), channel_id=1, source_target_pairs={{0,8},{8,16},{16,24},{24,32},{32,40},{40,48},{48,56},{56,64},{64,7... | collective-permute-start | bytes 786440 | tf_op jit(solution)/shard_map/ppermute | solution.py:21
  66.4 10.1 %collective-permute-start.9 = (bf16[4,16,16,128]{3,2,1,0:T(8,128)(2,1)}, bf16[4,16,16,128]{3,2,1,0:T(8,128)(2,1)S(1)}, u32[]{:S(2)}, u32[]{:S(2)}) collective-permute-start(bf16[4,16,16,128]{3,2,1,0:T(8,128)(2,1)} %convert_element_type.261), channel_id=1, source_target_pairs={{0,8},{8,16},{16,24},{24,32},{32,40},{40,48},{48,56},{56,64},{64,7... | collective-permute-start | bytes 786440 | tf_op jit(solution)/shard_map/ppermute | solution.py:21
  68.3 9.9 %collective-permute-start.8 = (bf16[4,16,16,128]{3,2,1,0:T(8,128)(2,1)}, bf16[4,16,16,128]{3,2,1,0:T(8,128)(2,1)S(1)}, u32[]{:S(2)}, u32[]{:S(2)}) collective-permute-start(bf16[4,16,16,128]{3,2,1,0:T(8,128)(2,1)} %convert_element_type.261), channel_id=1, source_target_pairs={{8,0},{16,8},{24,16},{32,24},{40,32},{48,40},{56,48},{64,56},{72,6... | collective-permute-start | bytes 786440 | tf_op jit(solution)/shard_map/ppermute | solution.py:22
  115.0 2.9 %copy-start.1 = (bf16[4,16,16,128]{3,2,1,0:T(8,128)(2,1)S(1)}, bf16[4,16,16,128]{3,2,1,0:T(8,128)(2,1)}, u32[]{:S(2)}) copy-start(bf16[4,16,16,128]{3,2,1,0:T(8,128)(2,1)} %convert_element_type.261) | copy-start | bytes 786436
  122.4 4.0 %collective-permute-start.10 = (f32[2,2,2,2,2,17,256]{6,4,5,3,2,1,0:T(2,128)}, f32[2,2,2,2,2,17,256]{6,4,5,3,2,1,0:T(2,128)S(1)}, u32[]{:S(2)}, u32[]{:S(2)}) collective-permute-start(f32[2,2,2,2,2,17,256]{6,4,5,3,2,1,0:T(2,128)} %copy.196), channel_id=1, source_target_pairs={{0,8},{8,0},{16,24},{24,16},{32,40},{40,32},{48,56},{56,48},{64,72... | collective-permute-start | bytes 1671176 | tf_op jit(solution)/shard_map/ppermute | solution.py:110
  127.0 10.6 %collective-permute-start.11 = (f32[2,2,2,2,17,256]{5,3,4,2,1,0:T(2,128)S(1)}, f32[2,2,2,2,17,256]{5,3,4,2,1,0:T(2,128)S(1)}, u32[]{:S(2)}, u32[]{:S(2)}) collective-permute-start(f32[2,2,2,2,17,256]{5,3,4,2,1,0:T(2,128)S(1)} %select_bitcast_fusion.1), channel_id=1, source_target_pairs={{0,16},{8,24},{16,0},{24,8},{32,48},{40,56},{48,32},{56,40},{64,80... | collective-permute-start | bytes 835592 | tf_op jit(solution)/shard_map/ppermute | solution.py:110
  138.1 10.7 %collective-permute-start.12 = (f32[2,2,2,17,256]{4,2,3,1,0:T(2,128)S(1)}, f32[2,2,2,17,256]{4,2,3,1,0:T(2,128)S(1)}, u32[]{:S(2)}, u32[]{:S(2)}) collective-permute-start(f32[2,2,2,17,256]{4,2,3,1,0:T(2,128)S(1)} %bitcast.109), channel_id=1, source_target_pairs={{0,32},{8,40},{16,48},{24,56},{32,0},{40,8},{48,16},{56,24},{64,96... | collective-permute-start | bytes 417800 | tf_op jit(solution)/shard_map/ppermute | solution.py:110
  149.1 10.2 %collective-permute-start.13 = (f32[2,2,17,256]{3,1,2,0:T(2,128)S(1)}, f32[2,2,17,256]{3,1,2,0:T(2,128)S(1)}, u32[]{:S(2)}, u32[]{:S(2)}) collective-permute-start(f32[2,2,17,256]{3,1,2,0:T(2,128)S(1)} %bitcast.110), channel_id=1, source_target_pairs={{0,64},{8,72},{16,80},{24,88},{32,96},{40,104},{48,112},{56,120},{... | collective-permute-start | bytes 208904 | tf_op jit(solution)/shard_map/ppermute | solution.py:110
  159.5 5.9 %collective-permute-start.14 = (f32[2,17,256]{2,0,1:T(2,128)S(1)}, f32[2,17,256]{2,0,1:T(2,128)S(1)}, u32[]{:S(2)}, u32[]{:S(2)}) collective-permute-start(f32[2,17,256]{2,0,1:T(2,128)S(1)} %bitcast.111), channel_id=1, source_target_pairs={{0,128},{8,136},{16,144},{24,152},{32,160},{40,168},{48,176},{56,1... | collective-permute-start | bytes 104456 | tf_op jit(solution)/shard_map/ppermute | solution.py:110
  165.5 7.2 %collective-permute-start.15 = (f32[17,256]{1,0:T(8,128)S(1)}, f32[17,256]{1,0:T(8,128)S(1)}, u32[]{:S(2)}, u32[]{:S(2)}) collective-permute-start(f32[17,256]{1,0:T(8,128)S(1)} %bitcast.112), channel_id=1, source_target_pairs={{0,256},{8,264},{16,272},{24,280},{32,288},{40,296},{48,304},{56,3... | collective-permute-start | bytes 52232 | tf_op jit(solution)/shard_map/ppermute | solution.py:110
Sparse Core Ops, SparseCore 0:
  66.4 46.3 all-gather.1
where the time goes:
time: 182 us; the launch traced here: 181 us
  waiting for transfers between devices  78.5 us (43%)
  starting transfers between devices  59.1 us (32%)
  between operations  14.6 us (8%)
  matrix products  11.8 us (6%)
  other arithmetic  11 us (6%)
  local copies, waits for them, and re-layouts  6.16 us (3%)
    all_gather x1, waiting for transfers between devices, on_device(): orbitals_all = lax.all_gather(rounded_orbitals, 'orb', axis=1, tiled=True)  34.1 us
    ppermute x6, starting transfers between devices, reduce_scatter_grid(): buf = keep + lax.ppermute(send, 'grid', pairs)  25.9 us
    ppermute x6, waiting for transfers between devices, reduce_scatter_grid(): buf = keep + lax.ppermute(send, 'grid', pairs)  22.7 us
    ppermute x5, starting transfers between devices, halo_layers(): after = lax.ppermute(initial, 'grid', down).astype(shard.dtype)  22.1 us
    ppermute x5, waiting for transfers between devices, halo_layers(): before = lax.ppermute(last, 'grid', up).astype(shard.dtype)  19.8 us
    ppermute x5, starting transfers between devices, halo_layers(): before = lax.ppermute(last, 'grid', up).astype(shard.dtype)  11 us
    dot_general x5, matrix products, apply_hamiltonian(): jnp.einsum('pq,zqo->zpo', plane, flat, precision=lax.Precision.HIGHEST, p...  10.4 us
  transfers between devices with their start and end apart: 17, of which 12 were waited for; matrix products, arithmetic and copies ran while one was open for 7% of the time, Pallas kernels for 0%

commit v1 on v0

--- a/solution.py
+++ b/solution.py
@@ -125,7 +125,15 @@
         .astype(jnp.bfloat16)
         .reshape(point_count, own_width)
     )
-    orbitals_all = lax.all_gather(rounded_orbitals, "orb", axis=1, tiled=True)
+    orbitals_all = jnp.concatenate(
+        jax.lax.all_to_all(
+            jnp.stack(tuple((rounded_orbitals for _ in range(jax.lax.axis_size("orb")))), axis=0),
+            "orb",
+            0,
+            0,
+        ),
+        axis=1,
+    )
     total_width = orbitals_all.shape[1]
     rows = total_width // grid_size
     hamiltonian_part = contract_points(orbitals_all, rounded_image)

time: 182 us -> 173 us (0.951)
  the two profiles are of different devices: /device:TPU:2 before, /device:TPU:6 now
where the time goes in v1:
time: 173 us; the launch traced here: 172 us
  waiting for transfers between devices  87.5 us (51%)
  starting transfers between devices  53.6 us (31%)
  matrix products  12.6 us (7%)
  other arithmetic  11.4 us (7%)
  local copies, waits for them, and re-layouts  6.04 us (3%)
    ppermute x6, waiting for transfers between devices, reduce_scatter_grid(): buf = keep + lax.ppermute(send, 'grid', pairs)  35.4 us
    all_to_all x1, waiting for transfers between devices, on_device(): jax.lax.all_to_all(jnp.stack(tuple((rounded_orbitals for _ in range(jax.l...  32.3 us
    ppermute x5, starting transfers between devices, halo_layers(): after = lax.ppermute(initial, 'grid', down).astype(shard.dtype)  22.3 us
    ppermute x5, waiting for transfers between devices, halo_layers(): before = lax.ppermute(last, 'grid', up).astype(shard.dtype)  19.8 us
    ppermute x6, starting transfers between devices, reduce_scatter_grid(): buf = keep + lax.ppermute(send, 'grid', pairs)  13.1 us
    dot_general x5, matrix products, apply_hamiltonian(): jnp.einsum('pq,zqo->zpo', plane, flat, precision=lax.Precision.HIGHEST, p...  11.2 us
    ppermute x5, starting transfers between devices, halo_layers(): before = lax.ppermute(last, 'grid', up).astype(shard.dtype)  11 us
    all_to_all x1, starting transfers between devices, on_device(): jax.lax.all_to_all(jnp.stack(tuple((rounded_orbitals for _ in range(jax.l...  7.1 us
  transfers between devices with their start and end apart: 17, of which 11 were waited for; matrix products, arithmetic and copies ran while one was open for 10% of the time, Pallas kernels for 0%

profile of v1, /device:TPU:6, one launch (start us, length us, event | category | flops | bytes accessed | tf_op | source)
XLA Modules:
  0.0 172.3 jit_solution(246250090848900902)
XLA Ops:
  1.7 10.7 %collective-permute-start = (bf16[4,16,16,128]{3,2,1,0:T(8,128)(2,1)S(1)}, bf16[4,16,16,128]{3,2,1,0:T(8,128)(2,1)S(1)}, u32[]{:S(2)}, u32[]{:S(2)}) collective-permute-start(bf16[4,16,16,128]{3,2,1,0:T(8,128)(2,1)S(1)} %convert_element_type.234), channel_id=1, source_target_pairs={{8,0},{16,8},{24,16},{32,24},{40,32},{48,40},{56,48},{64,56},{72,6... | collective-permute-start | bytes 786440 | tf_op jit(solution)/shard_map/ppermute | solution.py:22
  15.1 2.7 %fusion.102 = f32[256,4,128]{2,0,1:T(8,128)S(1)} fusion(f32[4,256,128]{2,1,0:T(8,128)} %bitcast.101, s32[256]{0:T(256)S(1)} %get-tuple-element.22, s32[256]{0:T(256)S(1)} %get-tuple-element.23), kind=kOutput, calls=%fused_computation.176 | convolution fusion | flops 408944640 | bytes 1050624 | tf_op jit(solution)/shard_map/pq,zqo->zpo/dot_general | solution.py:57
  17.9 4.3 %collective-permute-done.1 = bf16[4,16,16,128]{3,2,1,0:T(8,128)(2,1)S(1)} collective-permute-done((bf16[4,16,16,128]{3,2,1,0:T(8,128)(2,1)S(1)}, bf16[4,16,16,128]{3,2,1,0:T(8,128)(2,1)S(1)}, u32[]{:S(2)}, u32[]{:S(2)}) %collective-permute-start.1) | collective-permute-done | bytes 262176 | tf_op jit(solution)/shard_map/ppermute | solution.py:21
  24.6 2.4 %collective-permute-start.3 = (bf16[4,16,16,128]{3,2,1,0:T(8,128)(2,1)S(1)}, bf16[4,16,16,128]{3,2,1,0:T(8,128)(2,1)S(1)}, u32[]{:S(2)}, u32[]{:S(2)}) collective-permute-start(bf16[4,16,16,128]{3,2,1,0:T(8,128)(2,1)S(1)} %get-tuple-element.9), channel_id=1, source_target_pairs={{0,8},{8,16},{16,24},{24,32},{32,40},{40,48},{48,56},{56,64},{64,7... | collective-permute-start | bytes 786440 | tf_op jit(solution)/shard_map/ppermute | solution.py:21
  27.0 1.9 %convolution_bitcast_fusion.3 = f32[4,256,128]{1,2,0:T(8,128)S(1)} fusion(f32[4,256,128]{2,1,0:T(8,128)S(1)} %bitcast.106, s32[256]{0:T(256)S(1)} %get-tuple-element.22, s32[256]{0:T(256)S(1)} %get-tuple-element.23), kind=kOutput, calls=%fused_computation.44 | convolution fusion | flops 408944640 | bytes 1050624 | tf_op jit(solution)/shard_map/pq,zqo->zpo/dot_general | solution.py:57
  29.2 5.1 %collective-permute-done.3 = bf16[4,16,16,128]{3,2,1,0:T(8,128)(2,1)S(1)} collective-permute-done((bf16[4,16,16,128]{3,2,1,0:T(8,128)(2,1)S(1)}, bf16[4,16,16,128]{3,2,1,0:T(8,128)(2,1)S(1)}, u32[]{:S(2)}, u32[]{:S(2)}) %collective-permute-start.3) | collective-permute-done | bytes 262176 | tf_op jit(solution)/shard_map/ppermute | solution.py:21
  36.8 2.4 %collective-permute-start.5 = (bf16[4,16,16,128]{3,2,1,0:T(8,128)(2,1)S(1)}, bf16[4,16,16,128]{3,2,1,0:T(8,128)(2,1)S(1)}, u32[]{:S(2)}, u32[]{:S(2)}) collective-permute-start(bf16[4,16,16,128]{3,2,1,0:T(8,128)(2,1)S(1)} %get-tuple-element.7), channel_id=1, source_target_pairs={{0,8},{8,16},{16,24},{24,32},{32,40},{40,48},{48,56},{56,64},{64,7... | collective-permute-start | bytes 786440 | tf_op jit(solution)/shard_map/ppermute | solution.py:21
  39.2 1.9 %convolution_bitcast_fusion.2 = f32[4,256,128]{1,2,0:T(8,128)S(1)} fusion(f32[4,256,128]{2,1,0:T(8,128)S(1)} %bitcast.102, s32[256]{0:T(256)S(1)} %get-tuple-element.22, s32[256]{0:T(256)S(1)} %get-tuple-element.23), kind=kOutput, calls=%fused_computation.43 | convolution fusion | flops 408944640 | bytes 1050624 | tf_op jit(solution)/shard_map/pq,zqo->zpo/dot_general | solution.py:57
  41.4 5.2 %collective-permute-done.5 = bf16[4,16,16,128]{3,2,1,0:T(8,128)(2,1)S(1)} collective-permute-done((bf16[4,16,16,128]{3,2,1,0:T(8,128)(2,1)S(1)}, bf16[4,16,16,128]{3,2,1,0:T(8,128)(2,1)S(1)}, u32[]{:S(2)}, u32[]{:S(2)}) %collective-permute-start.5) | collective-permute-done | bytes 262176 | tf_op jit(solution)/shard_map/ppermute | solution.py:21
  49.0 2.4 %collective-permute-start.7 = (bf16[4,16,16,128]{3,2,1,0:T(8,128)(2,1)S(1)}, bf16[4,16,16,128]{3,2,1,0:T(8,128)(2,1)S(1)}, u32[]{:S(2)}, u32[]{:S(2)}) collective-permute-start(bf16[4,16,16,128]{3,2,1,0:T(8,128)(2,1)S(1)} %get-tuple-element.5), channel_id=1, source_target_pairs={{0,8},{8,16},{16,24},{24,32},{32,40},{40,48},{48,56},{56,64},{64,7... | collective-permute-start | bytes 786440 | tf_op jit(solution)/shard_map/ppermute | solution.py:21
  51.4 1.9 %convolution_bitcast_fusion.1 = f32[4,256,128]{1,2,0:T(8,128)S(1)} fusion(f32[4,256,128]{2,1,0:T(8,128)S(1)} %bitcast.111, s32[256]{0:T(256)S(1)} %get-tuple-element.22, s32[256]{0:T(256)S(1)} %get-tuple-element.23), kind=kOutput, calls=%fused_computation.42 | convolution fusion | flops 408944640 | bytes 1050624 | tf_op jit(solution)/shard_map/pq,zqo->zpo/dot_general | solution.py:57
  53.6 5.2 %collective-permute-done.7 = bf16[4,16,16,128]{3,2,1,0:T(8,128)(2,1)S(1)} collective-permute-done((bf16[4,16,16,128]{3,2,1,0:T(8,128)(2,1)S(1)}, bf16[4,16,16,128]{3,2,1,0:T(8,128)(2,1)S(1)}, u32[]{:S(2)}, u32[]{:S(2)}) %collective-permute-start.7) | collective-permute-done | bytes 262176 | tf_op jit(solution)/shard_map/ppermute | solution.py:21
  61.0 7.1 %all-to-all-start = ((bf16[8,1024,128]{1,2,0:T(8,128)(2,1)}), bf16[8,1024,128]{1,2,0:T(8,128)(2,1)S(1)}, u32[]{:S(2)}, u32[]{:S(2)}) async-start(bf16[8,1024,128]{1,2,0:T(8,128)(2,1)} %stack.3), calls=%async_computation | async-start | bytes 4194304 | tf_op jit(solution)/shard_map/all_to_all | solution.py:129
  70.1 5.9 %collective-permute-start.8 = (bf16[4,16,16,128]{3,2,1,0:T(8,128)(2,1)S(1)}, bf16[4,16,16,128]{3,2,1,0:T(8,128)(2,1)}, u32[]{:S(2)}, u32[]{:S(2)}) collective-permute-start(bf16[4,16,16,128]{3,2,1,0:T(8,128)(2,1)S(1)} %convert_element_type.262), channel_id=1, source_target_pairs={{8,0},{16,8},{24,16},{32,24},{40,32},{48,40},{56,48},{64,56},{72,6... | collective-permute-start | bytes 786440 | tf_op jit(solution)/shard_map/ppermute | solution.py:22
  76.1 2.7 %convolution_bitcast_fusion = f32[4,256,128]{1,2,0:T(8,128)} fusion(f32[4,256,128]{2,1,0:T(8,128)S(1)} %bitcast.100, s32[256]{0:T(256)S(1)} %get-tuple-element.22, s32[256]{0:T(256)S(1)} %get-tuple-element.23), kind=kOutput, calls=%fused_computation.41 | convolution fusion | flops 408944640 | bytes 1050624 | tf_op jit(solution)/shard_map/pq,zqo->zpo/dot_general | solution.py:57
  83.2 32.3 %all-to-all-done = bf16[8,1024,128]{1,2,0:T(8,128)(2,1)S(1)} async-done(((bf16[8,1024,128]{1,2,0:T(8,128)(2,1)}), bf16[8,1024,128]{1,2,0:T(8,128)(2,1)S(1)}, u32[]{:S(2)}, u32[]{:S(2)}) %all-to-all-start) | async-done | bytes 2097184 | tf_op jit(solution)/shard_map/all_to_all | solution.py:129
  122.4 2.1 %collective-permute-done.10 = f32[2,2,2,2,2,17,256]{6,4,5,3,2,1,0:T(2,128)S(1)} collective-permute-done((f32[2,2,2,2,2,17,256]{6,4,5,3,2,1,0:T(2,128)}, f32[2,2,2,2,2,17,256]{6,4,5,3,2,1,0:T(2,128)S(1)}, u32[]{:S(2)}, u32[]{:S(2)}) %collective-permute-start.10) | collective-permute-done | bytes 557088 | tf_op jit(solution)/shard_map/ppermute | solution.py:110
  127.1 8.7 %collective-permute-done.11 = f32[2,2,2,2,17,256]{5,3,4,2,1,0:T(2,128)S(1)} collective-permute-done((f32[2,2,2,2,17,256]{5,3,4,2,1,0:T(2,128)S(1)}, f32[2,2,2,2,17,256]{5,3,4,2,1,0:T(2,128)S(1)}, u32[]{:S(2)}, u32[]{:S(2)}) %collective-permute-start.11) | collective-permute-done | bytes 278560 | tf_op jit(solution)/shard_map/ppermute | solution.py:110
  138.3 8.7 %collective-permute-done.12 = f32[2,2,2,17,256]{4,2,3,1,0:T(2,128)S(1)} collective-permute-done((f32[2,2,2,17,256]{4,2,3,1,0:T(2,128)S(1)}, f32[2,2,2,17,256]{4,2,3,1,0:T(2,128)S(1)}, u32[]{:S(2)}, u32[]{:S(2)}) %collective-permute-start.12) | collective-permute-done | bytes 139296 | tf_op jit(solution)/shard_map/ppermute | solution.py:110
  149.2 8.2 %collective-permute-done.13 = f32[2,2,17,256]{3,1,2,0:T(2,128)S(1)} collective-permute-done((f32[2,2,17,256]{3,1,2,0:T(2,128)S(1)}, f32[2,2,17,256]{3,1,2,0:T(2,128)S(1)}, u32[]{:S(2)}, u32[]{:S(2)}) %collective-permute-start.13) | collective-permute-done | bytes 69664 | tf_op jit(solution)/shard_map/ppermute | solution.py:110
  157.5 2.4 %collective-permute-start.14 = (f32[2,17,256]{2,0,1:T(2,128)S(1)}, f32[2,17,256]{2,0,1:T(2,128)S(1)}, u32[]{:S(2)}, u32[]{:S(2)}) collective-permute-start(f32[2,17,256]{2,0,1:T(2,128)S(1)} %bitcast.116), channel_id=1, source_target_pairs={{0,128},{8,136},{16,144},{24,152},{32,160},{40,168},{48,176},{56,1... | collective-permute-start | bytes 104456 | tf_op jit(solution)/shard_map/ppermute | solution.py:110
  159.9 3.4 %collective-permute-done.14 = f32[2,17,256]{2,0,1:T(2,128)S(1)} collective-permute-done((f32[2,17,256]{2,0,1:T(2,128)S(1)}, f32[2,17,256]{2,0,1:T(2,128)S(1)}, u32[]{:S(2)}, u32[]{:S(2)}) %collective-permute-start.14) | collective-permute-done | bytes 34848 | tf_op jit(solution)/shard_map/ppermute | solution.py:110
  163.4 3.0 %collective-permute-start.15 = (f32[17,256]{1,0:T(8,128)S(1)}, f32[17,256]{1,0:T(8,128)S(1)}, u32[]{:S(2)}, u32[]{:S(2)}) collective-permute-start(f32[17,256]{1,0:T(8,128)S(1)} %bitcast.117), channel_id=1, source_target_pairs={{0,256},{8,264},{16,272},{24,280},{32,288},{40,296},{48,304},{56,3... | collective-permute-start | bytes 52232 | tf_op jit(solution)/shard_map/ppermute | solution.py:110
  166.4 4.2 %collective-permute-done.15 = f32[17,256]{1,0:T(8,128)S(1)} collective-permute-done((f32[17,256]{1,0:T(8,128)S(1)}, f32[17,256]{1,0:T(8,128)S(1)}, u32[]{:S(2)}, u32[]{:S(2)}) %collective-permute-start.15) | collective-permute-done | bytes 17440 | tf_op jit(solution)/shard_map/ppermute | solution.py:110
  (79 shorter events, 36.1 us)
Async XLA Ops:
  1.7 16.1 %collective-permute-start = (bf16[4,16,16,128]{3,2,1,0:T(8,128)(2,1)S(1)}, bf16[4,16,16,128]{3,2,1,0:T(8,128)(2,1)S(1)}, u32[]{:S(2)}, u32[]{:S(2)}) collective-permute-start(bf16[4,16,16,128]{3,2,1,0:T(8,128)(2,1)S(1)} %convert_element_type.234), channel_id=1, source_target_pairs={{8,0},{16,8},{24,16},{32,24},{40,32},{48,40},{56,48},{64,56},{72,6... | collective-permute-start | bytes 786440 | tf_op jit(solution)/shard_map/ppermute | solution.py:22
  12.4 9.8 %collective-permute-start.1 = (bf16[4,16,16,128]{3,2,1,0:T(8,128)(2,1)S(1)}, bf16[4,16,16,128]{3,2,1,0:T(8,128)(2,1)S(1)}, u32[]{:S(2)}, u32[]{:S(2)}) collective-permute-start(bf16[4,16,16,128]{3,2,1,0:T(8,128)(2,1)S(1)} %convert_element_type.234), channel_id=1, source_target_pairs={{0,8},{8,16},{16,24},{24,32},{32,40},{40,48},{48,56},{56,64},{64,7... | collective-permute-start | bytes 786440 | tf_op jit(solution)/shard_map/ppermute | solution.py:21
  15.1 7.1 %copy-start = (f32[4,16,16,128]{3,2,1,0:T(8,128)S(1)}, f32[4,16,16,128]{3,2,1,0:T(8,128)}, u32[]{:S(2)}) copy-start(f32[4,16,16,128]{3,2,1,0:T(8,128)} %param.2) | copy-start | bytes 1572868
  15.1 7.1 %copy-start.2 = (f32[4,16,16]{2,1,0:T(8,128)S(1)}, f32[4,16,16]{2,1,0:T(8,128)}, u32[]{:S(2)}) copy-start(f32[4,16,16]{2,1,0:T(8,128)} %param.3) | copy-start | bytes 12292
  22.6 6.5 %collective-permute-start.2 = (bf16[4,16,16,128]{3,2,1,0:T(8,128)(2,1)S(1)}, bf16[4,16,16,128]{3,2,1,0:T(8,128)(2,1)S(1)}, u32[]{:S(2)}, u32[]{:S(2)}) collective-permute-start(bf16[4,16,16,128]{3,2,1,0:T(8,128)(2,1)S(1)} %get-tuple-element.9), channel_id=1, source_target_pairs={{8,0},{16,8},{24,16},{32,24},{40,32},{48,40},{56,48},{64,56},{72,6... | collective-permute-start | bytes 786440 | tf_op jit(solution)/shard_map/ppermute | solution.py:22
  24.6 9.8 %collective-permute-start.3 = (bf16[4,16,16,128]{3,2,1,0:T(8,128)(2,1)S(1)}, bf16[4,16,16,128]{3,2,1,0:T(8,128)(2,1)S(1)}, u32[]{:S(2)}, u32[]{:S(2)}) collective-permute-start(bf16[4,16,16,128]{3,2,1,0:T(8,128)(2,1)S(1)} %get-tuple-element.9), channel_id=1, source_target_pairs={{0,8},{8,16},{16,24},{24,32},{32,40},{40,48},{48,56},{56,64},{64,7... | collective-permute-start | bytes 786440 | tf_op jit(solution)/shard_map/ppermute | solution.py:21
  34.8 6.5 %collective-permute-start.4 = (bf16[4,16,16,128]{3,2,1,0:T(8,128)(2,1)S(1)}, bf16[4,16,16,128]{3,2,1,0:T(8,128)(2,1)S(1)}, u32[]{:S(2)}, u32[]{:S(2)}) collective-permute-start(bf16[4,16,16,128]{3,2,1,0:T(8,128)(2,1)S(1)} %get-tuple-element.7), channel_id=1, source_target_pairs={{8,0},{16,8},{24,16},{32,24},{40,32},{48,40},{56,48},{64,56},{72,6... | collective-permute-start | bytes 786440 | tf_op jit(solution)/shard_map/ppermute | solution.py:22
  36.8 9.8 %collective-permute-start.5 = (bf16[4,16,16,128]{3,2,1,0:T(8,128)(2,1)S(1)}, bf16[4,16,16,128]{3,2,1,0:T(8,128)(2,1)S(1)}, u32[]{:S(2)}, u32[]{:S(2)}) collective-permute-start(bf16[4,16,16,128]{3,2,1,0:T(8,128)(2,1)S(1)} %get-tuple-element.7), channel_id=1, source_target_pairs={{0,8},{8,16},{16,24},{24,32},{32,40},{40,48},{48,56},{56,64},{64,7... | collective-permute-start | bytes 786440 | tf_op jit(solution)/shard_map/ppermute | solution.py:21
  47.0 6.5 %collective-permute-start.6 = (bf16[4,16,16,128]{3,2,1,0:T(8,128)(2,1)S(1)}, bf16[4,16,16,128]{3,2,1,0:T(8,128)(2,1)S(1)}, u32[]{:S(2)}, u32[]{:S(2)}) collective-permute-start(bf16[4,16,16,128]{3,2,1,0:T(8,128)(2,1)S(1)} %get-tuple-element.5), channel_id=1, source_target_pairs={{8,0},{16,8},{24,16},{32,24},{40,32},{48,40},{56,48},{64,56},{72,6... | collective-permute-start | bytes 786440 | tf_op jit(solution)/shard_map/ppermute | solution.py:22
  49.0 9.8 %collective-permute-start.7 = (bf16[4,16,16,128]{3,2,1,0:T(8,128)(2,1)S(1)}, bf16[4,16,16,128]{3,2,1,0:T(8,128)(2,1)S(1)}, u32[]{:S(2)}, u32[]{:S(2)}) collective-permute-start(bf16[4,16,16,128]{3,2,1,0:T(8,128)(2,1)S(1)} %get-tuple-element.5), channel_id=1, source_target_pairs={{0,8},{8,16},{16,24},{24,32},{32,40},{40,48},{48,56},{56,64},{64,7... | collective-permute-start | bytes 786440 | tf_op jit(solution)/shard_map/ppermute | solution.py:21
  61.0 54.4 %all-to-all-start = ((bf16[8,1024,128]{1,2,0:T(8,128)(2,1)}), bf16[8,1024,128]{1,2,0:T(8,128)(2,1)S(1)}, u32[]{:S(2)}, u32[]{:S(2)}) async-start(bf16[8,1024,128]{1,2,0:T(8,128)(2,1)} %stack.3), calls=%async_computation | async-start | bytes 4194304 | tf_op jit(solution)/shard_map/all_to_all | solution.py:129
  68.2 11.9 %collective-permute-start.9 = (bf16[4,16,16,128]{3,2,1,0:T(8,128)(2,1)S(1)}, bf16[4,16,16,128]{3,2,1,0:T(8,128)(2,1)}, u32[]{:S(2)}, u32[]{:S(2)}) collective-permute-start(bf16[4,16,16,128]{3,2,1,0:T(8,128)(2,1)S(1)} %convert_element_type.262), channel_id=1, source_target_pairs={{0,8},{8,16},{16,24},{24,32},{32,40},{40,48},{48,56},{56,64},{64,7... | collective-permute-start | bytes 786440 | tf_op jit(solution)/shard_map/ppermute | solution.py:21
  70.1 11.0 %collective-permute-start.8 = (bf16[4,16,16,128]{3,2,1,0:T(8,128)(2,1)S(1)}, bf16[4,16,16,128]{3,2,1,0:T(8,128)(2,1)}, u32[]{:S(2)}, u32[]{:S(2)}) collective-permute-start(bf16[4,16,16,128]{3,2,1,0:T(8,128)(2,1)S(1)} %convert_element_type.262), channel_id=1, source_target_pairs={{8,0},{16,8},{24,16},{32,24},{40,32},{48,40},{56,48},{64,56},{72,6... | collective-permute-start | bytes 786440 | tf_op jit(solution)/shard_map/ppermute | solution.py:22
  83.2 33.6 %copy-start.1 = (bf16[4,16,16,128]{3,2,1,0:T(8,128)(2,1)S(1)}, bf16[4,16,16,128]{3,2,1,0:T(8,128)(2,1)}, u32[]{:S(2)}) copy-start(bf16[4,16,16,128]{3,2,1,0:T(8,128)(2,1)} %fusion.9) | copy-start | bytes 786436
  120.5 4.0 %collective-permute-start.10 = (f32[2,2,2,2,2,17,256]{6,4,5,3,2,1,0:T(2,128)}, f32[2,2,2,2,2,17,256]{6,4,5,3,2,1,0:T(2,128)S(1)}, u32[]{:S(2)}, u32[]{:S(2)}) collective-permute-start(f32[2,2,2,2,2,17,256]{6,4,5,3,2,1,0:T(2,128)} %copy.196), channel_id=1, source_target_pairs={{0,8},{8,0},{16,24},{24,16},{32,40},{40,32},{48,56},{56,48},{64,72... | collective-permute-start | bytes 1671176 | tf_op jit(solution)/shard_map/ppermute | solution.py:110
  125.2 10.6 %collective-permute-start.11 = (f32[2,2,2,2,17,256]{5,3,4,2,1,0:T(2,128)S(1)}, f32[2,2,2,2,17,256]{5,3,4,2,1,0:T(2,128)S(1)}, u32[]{:S(2)}, u32[]{:S(2)}) collective-permute-start(f32[2,2,2,2,17,256]{5,3,4,2,1,0:T(2,128)S(1)} %select_bitcast_fusion.1), channel_id=1, source_target_pairs={{0,16},{8,24},{16,0},{24,8},{32,48},{40,56},{48,32},{56,40},{64,80... | collective-permute-start | bytes 835592 | tf_op jit(solution)/shard_map/ppermute | solution.py:110
  136.3 10.7 %collective-permute-start.12 = (f32[2,2,2,17,256]{4,2,3,1,0:T(2,128)S(1)}, f32[2,2,2,17,256]{4,2,3,1,0:T(2,128)S(1)}, u32[]{:S(2)}, u32[]{:S(2)}) collective-permute-start(f32[2,2,2,17,256]{4,2,3,1,0:T(2,128)S(1)} %bitcast.114), channel_id=1, source_target_pairs={{0,32},{8,40},{16,48},{24,56},{32,0},{40,8},{48,16},{56,24},{64,96... | collective-permute-start | bytes 417800 | tf_op jit(solution)/shard_map/ppermute | solution.py:110
  147.3 10.1 %collective-permute-start.13 = (f32[2,2,17,256]{3,1,2,0:T(2,128)S(1)}, f32[2,2,17,256]{3,1,2,0:T(2,128)S(1)}, u32[]{:S(2)}, u32[]{:S(2)}) collective-permute-start(f32[2,2,17,256]{3,1,2,0:T(2,128)S(1)} %bitcast.115), channel_id=1, source_target_pairs={{0,64},{8,72},{16,80},{24,88},{32,96},{40,104},{48,112},{56,120},{... | collective-permute-start | bytes 208904 | tf_op jit(solution)/shard_map/ppermute | solution.py:110
  157.5 5.8 %collective-permute-start.14 = (f32[2,17,256]{2,0,1:T(2,128)S(1)}, f32[2,17,256]{2,0,1:T(2,128)S(1)}, u32[]{:S(2)}, u32[]{:S(2)}) collective-permute-start(f32[2,17,256]{2,0,1:T(2,128)S(1)} %bitcast.116), channel_id=1, source_target_pairs={{0,128},{8,136},{16,144},{24,152},{32,160},{40,168},{48,176},{56,1... | collective-permute-start | bytes 104456 | tf_op jit(solution)/shard_map/ppermute | solution.py:110
  163.4 7.2 %collective-permute-start.15 = (f32[17,256]{1,0:T(8,128)S(1)}, f32[17,256]{1,0:T(8,128)S(1)}, u32[]{:S(2)}, u32[]{:S(2)}) collective-permute-start(f32[17,256]{1,0:T(8,128)S(1)} %bitcast.117), channel_id=1, source_target_pairs={{0,256},{8,264},{16,272},{24,280},{32,288},{40,296},{48,304},{56,3... | collective-permute-start | bytes 52232 | tf_op jit(solution)/shard_map/ppermute | solution.py:110
